TPU v7x, 128 devices: a whole 4x4x4 slice. The times are simulated.
128 devices in a mesh: mode: 8 (over x, core), member: 16 (over z, y).
Axes of the slice: x: 4, y: 4, z: 4, core: 2. Of those that a mesh axis runs over, the one named last changes fastest.
Arguments:
- ground_accel: bfloat16 [4, 639], replicated, may hold values from -6 to 6
- modal_kernel: bfloat16 [4096, 512], P(('mode', 'member')), may hold values from -0.25 to 0.25
- mode_shapes: bfloat16 [98304, 4096], P('member', 'mode'), may hold values from -0.09375 to 0.09375
- member_owner: int32 [16384, 1], P('member'), may hold values from 0 to 127; in each aligned block of 128 rows (0 to 127, 128 to 255, ...) at most 2 rows name the same one
- member_group: int32 [16384, 1], P('member'), may hold values from 0 to 3
- record_table: int32 [512, 8], P(('mode', 'member')), may hold values from 0 to 3
- case_coef: float32 [8, 6], replicated, may hold values from -1.5 to 1.5
- gravity: float32 [512, 8], P(('mode', 'member')), may hold values from -10 to 10
Outputs:
- demand: float32 [512, 8], P(('mode', 'member'))
Inputs may be any that keep to these rules, and one draw needn't show every extreme that they name: `member_owner`: in each aligned block of 1024 / 8 members no owner is named more than 2 times, a bound that some block reaches.
All inputs are finite; a program needn't handle non-finite values.
Results may differ from a plain program's by a relative error of at most 0.0065.
Values may be sent and summed in bfloat16 or wider, within the bound.
No kernel may reach another device: no remote copies, remote signals or barrier semaphores. Data moves between devices by JAX's collectives and lax.ppermute only.
A program may use at most 64 MiB of HBM per device.

v0:
```python
import jax
import jax.numpy as jnp
from jax import lax
from jax.sharding import PartitionSpec as P


def lagged_table(ground_accel, tap_count):
    record_count, span_len = ground_accel.shape
    step_count = span_len - tap_count + 1
    offsets = tap_count - 1 + jnp.arange(step_count)[None, :] - jnp.arange(tap_count)[:, None]
    lag_table = ground_accel[:, offsets]
    return jnp.transpose(lag_table, (1, 0, 2)).reshape(tap_count, record_count * step_count)


def local(
    ground_accel,
    modal_kernel,
    mode_shapes,
    member_owner,
    member_group,
    record_table,
    case_coef,
    gravity,
):
    tap_count = modal_kernel.shape[1]
    record_count = ground_accel.shape[0]
    comp_count = case_coef.shape[1]
    group_count = gravity.shape[0]
    n_mode = lax.axis_size("mode")
    n_member = lax.axis_size("member")
    lagged = lagged_table(ground_accel, tap_count)
    local_resp = jnp.dot(modal_kernel, lagged, preferred_element_type=jnp.float32).astype(
        jnp.bfloat16
    )
    modal_resp = lax.all_gather(local_resp, "member", axis=0, tiled=True)
    own_rows = mode_shapes.shape[0] // n_mode
    forces = lax.psum_scatter(
        jnp.dot(mode_shapes, modal_resp, preferred_element_type=jnp.float32).astype(jnp.bfloat16),
        "mode",
        scatter_dimension=0,
        tiled=True,
    ).astype(jnp.float32)
    members_here = own_rows // comp_count
    owner_total = n_mode * n_member
    slot_depth = max(2, 2 * members_here // owner_total)
    packed = forces.reshape(members_here, comp_count * forces.shape[1])
    first_row = lax.axis_index("mode") * members_here
    owner_ids = lax.dynamic_slice_in_dim(member_owner[:, 0], first_row, members_here)
    group_ids = lax.dynamic_slice_in_dim(member_group[:, 0], first_row, members_here)
    position = jnp.arange(members_here)
    earlier = (owner_ids[:, None] == owner_ids[None, :]) & (position[None, :] < position[:, None])
    member_rank = jnp.sum(earlier.astype(jnp.int32), axis=1)
    slot_index = owner_ids * slot_depth + member_rank
    slot_total = owner_total * slot_depth
    placement = jnp.arange(slot_total)[:, None] == slot_index[None, :]
    outgoing = jnp.dot(placement.astype(jnp.float32), packed, precision=lax.Precision.HIGHEST)
    slot_labels = jnp.max(jnp.where(placement, group_ids[None, :], -1), axis=1)
    incoming, slot_tags = (
        lax.all_to_all(
            outgoing.reshape(owner_total, slot_depth, -1).astype(jnp.bfloat16),
            ("mode", "member"),
            split_axis=0,
            concat_axis=0,
            tiled=True,
        ).astype(jnp.float32),
        lax.all_to_all(
            slot_labels.reshape(owner_total, slot_depth),
            ("mode", "member"),
            split_axis=0,
            concat_axis=0,
            tiled=True,
        ),
    )
    selector = (jnp.arange(group_count)[:, None] == slot_tags.reshape(-1)[None, :]).astype(
        jnp.float32
    )
    group_sums = jnp.dot(
        selector, incoming.reshape(selector.shape[1], -1), precision=lax.Precision.HIGHEST
    )
    group_sums = group_sums.reshape(group_count, comp_count, record_count, -1)
    case_mix = jnp.einsum("sc,gcrt->gsrt", case_coef, group_sums, precision=lax.Precision.HIGHEST)
    record_pick = (record_table[:, :, None] == jnp.arange(record_count)[None, None, :]).astype(
        jnp.float32
    )
    selected = jnp.sum(record_pick[:, :, :, None] * case_mix, axis=2)
    combined = gravity[:, :, None] + selected
    return jnp.max(jnp.abs(combined), axis=2)


def solution(mesh):
    placed = (
        P(),
        P(("mode", "member"), None),
        P("member", "mode"),
        P("member", None),
        P("member", None),
        P(("mode", "member"), None),
        P(),
        P(("mode", "member"), None),
    )
    return jax.shard_map(
        local, mesh=mesh, in_specs=placed, out_specs=P(("mode", "member"), None), check_vma=False
    )
```

profile of v0, /device:TPU:1, one launch (start us, length us, event | category | flops | bytes accessed | tf_op | source)
XLA Modules:
  0.0 376.7 jit_solution(7160551659993161368)
XLA Ops:
  6.5 0.9 copy.22
  7.5 227.3 %gather_fusion = bf16[65536,4]{1,0:T(8,128)(2,1)} fusion(bf16[4,639]{0,1:T(8,128)(2,1)S(1)} %copy.22, s32[65536]{0:T(1024)S(1)} %fusion.5), kind=kCustom, calls=%fused_computation | custom fusion | bytes 1310720 | tf_op jit(solution)/shard_map/gather | solution.py:11
  234.8 17.2 %copy.23 = bf16[512,128,4]{0,1,2:T(8,128)(2,1)S(1)} copy(bf16[512,128,4]{2,1,0:T(8,128)(2,1)} %bitcast.43) | data formatting | bytes 1048576 | tf_op jit(solution)/shard_map/gather | solution.py:11
  252.1 0.2 fusion.3
  252.3 21.2 %all_gather.3 = bf16[512,512]{1,0:T(8,128)(2,1)S(1)} all-gather(bf16[32,512]{1,0:T(8,128)(2,1)S(1)} %fusion.3), channel_id=1, replica_groups=mesh['mode'=8,'member'=16] {'member'}, dimensions={0}, use_global_device_ids=true | all-gather | bytes 557056 | tf_op jit(solution)/shard_map/all_gather | solution.py:35
  273.5 8.3 %fusion = bf16[6144,512]{0,1:T(8,128)(2,1)} fusion(bf16[512,512]{1,0:T(8,128)(2,1)S(1)} %all_gather.3, bf16[6144,512]{1,0:T(8,128)(2,1)} %param.10), kind=kOutput, calls=%fused_computation.2 | convolution fusion | flops 3224371200 | bytes 13107200 | tf_op jit(solution)/shard_map/dot_general | solution.py:38
  281.8 0.7 dynamic-slice_bitcast_fusion.1
  282.5 0.7 dynamic-slice_bitcast_fusion
  283.3 0.7 multiply_add_fusion.1
  284.1 0.8 all_to_all.9
  284.8 12.8 %all-to-all-start = ((s32[128,1,2]{2,1,0:T(1,128)}), s32[128,1,2]{2,1,0:T(1,128)S(1)}, u32[]{:S(2)}, u32[]{:S(2)}) async-start(s32[128,1,2]{2,1,0:T(1,128)} %bitcast.2), calls=%async_computation | async-start | bytes 131072 | tf_op jit(solution)/shard_map/all_to_all | solution.py:66
  297.6 31.4 %reduce-scatter.2.cloned.1.call-done = bf16[768,512]{0,1:T(8,128)(2,1)} async-done(((bf16[6144,512]{0,1:T(8,128)(2,1)}), bf16[768,512]{0,1:T(8,128)(2,1)}) %reduce-scatter.2.cloned.1.call-update) | async-done | bytes 786448 | tf_op jit(solution)/shard_map/reduce_scatter | solution.py:37
  329.0 1.4 copy.24
  330.4 0.7 reshape.112
  331.1 0.6 convolution_convert_fusion.1
  331.7 2.8 copy.25
  334.5 8.5 %all-to-all-start.1 = ((bf16[128,2,3072]{2,1,0:T(2,128)(2,1)}), bf16[128,2,3072]{2,1,0:T(2,128)(2,1)S(1)}, u32[]{:S(2)}, u32[]{:S(2)}) async-start(bf16[128,2,3072]{2,1,0:T(2,128)(2,1)} %copy.25), calls=%async_computation.2 | async-start | bytes 3145728 | tf_op jit(solution)/shard_map/all_to_all | solution.py:59
  343.0 0.5 broadcast.73
  343.5 0.8 reduce.3
  344.5 22.6 %all-to-all-done.1 = bf16[128,2,3072]{2,1,0:T(2,128)(2,1)S(1)} async-done(((bf16[128,2,3072]{2,1,0:T(2,128)(2,1)}), bf16[128,2,3072]{2,1,0:T(2,128)(2,1)S(1)}, u32[]{:S(2)}, u32[]{:S(2)}) %all-to-all-start.1) | async-done | bytes 1572896 | tf_op jit(solution)/shard_map/all_to_all | solution.py:59
  367.1 0.6 reshape.102
  367.7 0.7 copy.26
  368.4 0.5 fusion.14
  369.2 0.7 abs_reduce_fusion
  (19 shorter events, 0.8 us)
Async XLA Ops:
  6.5 245.6 %copy-start = (bf16[32,512]{1,0:T(8,128)(2,1)S(1)}, bf16[32,512]{1,0:T(8,128)(2,1)}, u32[]{:S(2)}) copy-start(bf16[32,512]{1,0:T(8,128)(2,1)} %param.9) | copy-start | bytes 98308
  6.5 322.5 %reduce-scatter.2.cloned.1.call-start = ((), (), s32[]{:S(2)}) async-start(), calls=%async_computation.3 | async-start | bytes 7077888 | tf_op jit(solution)/shard_map/reduce_scatter | solution.py:37
  281.8 61.2 %copy-start.1 = (s32[4,8]{1,0:T(4,128)S(1)}, s32[4,8]{1,0:T(4,128)}, u32[]{:S(2)}) copy-start(s32[4,8]{1,0:T(4,128)} %param.13) | copy-start | bytes 388
  284.8 49.6 %all-to-all-start = ((s32[128,1,2]{2,1,0:T(1,128)}), s32[128,1,2]{2,1,0:T(1,128)S(1)}, u32[]{:S(2)}, u32[]{:S(2)}) async-start(s32[128,1,2]{2,1,0:T(1,128)} %bitcast.2), calls=%async_computation | async-start | bytes 131072 | tf_op jit(solution)/shard_map/all_to_all | solution.py:66
  334.5 34.5 %copy-start.3 = (f32[8,6]{1,0:T(8,128)S(1)}, f32[8,6]{1,0:T(8,128)}, u32[]{:S(2)}) copy-start(f32[8,6]{1,0:T(8,128)} %param.14) | copy-start | bytes 580
  334.5 34.7 %copy-start.2 = (f32[4,8]{1,0:T(4,128)S(1)}, f32[4,8]{1,0:T(4,128)}, u32[]{:S(2)}) copy-start(f32[4,8]{1,0:T(4,128)} %param.15) | copy-start | bytes 388
  334.5 32.6 %all-to-all-start.1 = ((bf16[128,2,3072]{2,1,0:T(2,128)(2,1)}), bf16[128,2,3072]{2,1,0:T(2,128)(2,1)S(1)}, u32[]{:S(2)}, u32[]{:S(2)}) async-start(bf16[128,2,3072]{2,1,0:T(2,128)(2,1)} %copy.25), calls=%async_computation.2 | async-start | bytes 3145728 | tf_op jit(solution)/shard_map/all_to_all | solution.py:59
Sparse Core Ops, SparseCore 0:
  281.9 47.0 reduce-scatter.1
where the time goes:
time: 377 us
  local copies, waits for them, and re-layouts  254 us (67%)
  waiting for transfers between devices  54 us (14%)
  starting transfers between devices  21.3 us (6%)
  blocking collectives  21.2 us (6%)
  between operations  13.5 us (4%)
  matrix products  9.81 us (3%)
    gather x2, local copies, waits for them, and re-layouts, lagged_table(): lag_table = ground_accel[:, offsets]  245 us
    reduce_scatter x1, waiting for transfers between devices, local(): lax.psum_scatter(jnp.dot(mode_shapes, modal_resp, preferred_element_type=...  31.4 us
    all_to_all x1, waiting for transfers between devices, local(): lax.all_to_all(outgoing.reshape(owner_total, slot_depth, -1).astype(jnp.b...  22.6 us
    all_gather x1, blocking collectives, local(): modal_resp = lax.all_gather(local_resp, 'member', axis=0, tiled=True)  21.2 us
    all_to_all x1, starting transfers between devices, local(): lax.all_to_all(slot_labels.reshape(owner_total, slot_depth), ('mode', 'me...  12.8 us
    all_to_all x1, starting transfers between devices, local(): lax.all_to_all(outgoing.reshape(owner_total, slot_depth, -1).astype(jnp.b...  8.53 us
    dot_general x1, matrix products, local(): jnp.dot(mode_shapes, modal_resp, preferred_element_type=jnp.float32)  8.25 us
  transfers between devices with their start and end apart: 3, of which 2 were waited for; matrix products, arithmetic and copies ran while one was open for 2% of the time, Pallas kernels for 0%

commit v1 on v0

--- a/solution.py
+++ b/solution.py
@@ -32,7 +32,11 @@
     local_resp = jnp.dot(modal_kernel, lagged, preferred_element_type=jnp.float32).astype(
         jnp.bfloat16
     )
-    modal_resp = lax.all_gather(local_resp, "member", axis=0, tiled=True)
+    size = lax.axis_size("member")
+    repeats = [size if d == 0 else 1 for d in range(local_resp.ndim)]
+    modal_resp = lax.all_to_all(
+        jnp.tile(local_resp, repeats), "member", split_axis=0, concat_axis=0, tiled=True
+    )
     own_rows = mode_shapes.shape[0] // n_mode
     forces = lax.psum_scatter(
         jnp.dot(mode_shapes, modal_resp, preferred_element_type=jnp.float32).astype(jnp.bfloat16),

time: 377 us -> 370 us (0.981)
  starting transfers between devices: 21.3 us -> 15.6 us
    all_gather x1 -> x0, blocking collectives: 21.2 us -> none  [local(): modal_resp = lax.all_gather(local_resp, 'member', axis=0, tiled=True)]
    all_to_all x0 -> x1, blocking collectives: none -> 18.9 us  [local(): lax.all_to_all(jnp.tile(local_resp, repeats), 'member', split_axis=0, con...]
    all_to_all x1, starting transfers between devices: 12.8 us -> 7.07 us  [local(): lax.all_to_all(slot_labels.reshape(owner_total, slot_depth), ('mode', 'me...]
where the time goes in v1:
time: 370 us; the launch traced here: 369 us
  local copies, waits for them, and re-layouts  254 us (69%)
  waiting for transfers between devices  54 us (15%)
  blocking collectives  18.9 us (5%)
  starting transfers between devices  15.6 us (4%)
  between operations  13.5 us (4%)
  matrix products  9.81 us (3%)
    gather x2, local copies, waits for them, and re-layouts, lagged_table(): lag_table = ground_accel[:, offsets]  245 us
    reduce_scatter x1, waiting for transfers between devices, local(): lax.psum_scatter(jnp.dot(mode_shapes, modal_resp, preferred_element_type=...  31.4 us
    all_to_all x1, waiting for transfers between devices, local(): lax.all_to_all(outgoing.reshape(owner_total, slot_depth, -1).astype(jnp.b...  22.6 us
    all_to_all x1, blocking collectives, local(): lax.all_to_all(jnp.tile(local_resp, repeats), 'member', split_axis=0, con...  18.9 us
    all_to_all x1, starting transfers between devices, local(): lax.all_to_all(outgoing.reshape(owner_total, slot_depth, -1).astype(jnp.b...  8.5 us
    dot_general x1, matrix products, local(): jnp.dot(mode_shapes, modal_resp, preferred_element_type=jnp.float32)  8.24 us
  transfers between devices with their start and end apart: 3, of which 2 were waited for; matrix products, arithmetic and copies ran while one was open for 2% of the time, Pallas kernels for 0%

profile of v1, /device:TPU:1, one launch (start us, length us, event | category | flops | bytes accessed | tf_op | source)
XLA Modules:
  0.0 368.8 jit_solution(18380344585858045743)
XLA Ops:
  6.5 0.9 copy.22
  7.5 227.3 %gather_fusion = bf16[65536,4]{1,0:T(8,128)(2,1)} fusion(bf16[4,639]{0,1:T(8,128)(2,1)S(1)} %copy.22, s32[65536]{0:T(1024)S(1)} %fusion.5), kind=kCustom, calls=%fused_computation | custom fusion | bytes 1310720 | tf_op jit(solution)/shard_map/gather | solution.py:11
  234.8 17.2 %copy.23 = bf16[512,128,4]{0,1,2:T(8,128)(2,1)S(1)} copy(bf16[512,128,4]{2,1,0:T(8,128)(2,1)} %bitcast.44) | data formatting | bytes 1048576 | tf_op jit(solution)/shard_map/gather | solution.py:11
  252.1 0.2 fusion.3
  252.4 18.9 %all_to_all.23 = bf16[16,32,512]{2,1,0:T(8,128)(2,1)S(1)} all-to-all(bf16[16,32,512]{2,1,0:T(8,128)(2,1)S(1)} %tile.2), channel_id=1, replica_groups=mesh['mode'=8,'member'=16] {'member'}, dimensions={0} | all-to-all | bytes 1048576 | tf_op jit(solution)/shard_map/all_to_all | solution.py:37
  271.3 8.2 %fusion = bf16[6144,512]{0,1:T(8,128)(2,1)} fusion(bf16[512,512]{1,0:T(8,128)(2,1)S(1)} %bitcast.48, bf16[6144,512]{1,0:T(8,128)(2,1)} %param.10), kind=kOutput, calls=%fused_computation.2 | convolution fusion | flops 3224371200 | bytes 13107200 | tf_op jit(solution)/shard_map/dot_general | solution.py:42
  279.6 0.7 dynamic-slice_bitcast_fusion.1
  280.3 0.7 dynamic-slice_bitcast_fusion
  281.1 0.7 multiply_add_fusion.1
  281.9 0.8 all_to_all.15
  282.6 7.1 %all-to-all-start = ((s32[128,1,2]{2,1,0:T(1,128)}), s32[128,1,2]{2,1,0:T(1,128)S(1)}, u32[]{:S(2)}, u32[]{:S(2)}) async-start(s32[128,1,2]{2,1,0:T(1,128)} %bitcast.2), calls=%async_computation | async-start | bytes 131072 | tf_op jit(solution)/shard_map/all_to_all | solution.py:70
  289.7 31.4 %reduce-scatter.2.cloned.1.call-done = bf16[768,512]{0,1:T(8,128)(2,1)} async-done(((bf16[6144,512]{0,1:T(8,128)(2,1)}), bf16[768,512]{0,1:T(8,128)(2,1)}) %reduce-scatter.2.cloned.1.call-update) | async-done | bytes 786448 | tf_op jit(solution)/shard_map/reduce_scatter | solution.py:41
  321.1 1.4 copy.24
  322.5 0.7 reshape.119
  323.2 0.6 convolution_convert_fusion.1
  323.8 2.8 copy.25
  326.6 8.5 %all-to-all-start.2 = ((bf16[128,2,3072]{2,1,0:T(2,128)(2,1)}), bf16[128,2,3072]{2,1,0:T(2,128)(2,1)S(1)}, u32[]{:S(2)}, u32[]{:S(2)}) async-start(bf16[128,2,3072]{2,1,0:T(2,128)(2,1)} %copy.25), calls=%async_computation.3 | async-start | bytes 3145728 | tf_op jit(solution)/shard_map/all_to_all | solution.py:63
  335.1 0.5 broadcast.76
  335.7 0.8 reduce.3
  336.6 22.6 %all-to-all-done.2 = bf16[128,2,3072]{2,1,0:T(2,128)(2,1)S(1)} async-done(((bf16[128,2,3072]{2,1,0:T(2,128)(2,1)}), bf16[128,2,3072]{2,1,0:T(2,128)(2,1)S(1)}, u32[]{:S(2)}, u32[]{:S(2)}) %all-to-all-start.2) | async-done | bytes 1572896 | tf_op jit(solution)/shard_map/all_to_all | solution.py:63
  359.2 0.6 reshape.109
  359.8 0.7 copy.26
  360.5 0.5 fusion.14
  361.3 0.7 abs_reduce_fusion
  (20 shorter events, 0.8 us)
Async XLA Ops:
  6.5 245.6 %copy-start = (bf16[32,512]{1,0:T(8,128)(2,1)S(1)}, bf16[32,512]{1,0:T(8,128)(2,1)}, u32[]{:S(2)}) copy-start(bf16[32,512]{1,0:T(8,128)(2,1)} %param.9) | copy-start | bytes 98308
  6.5 314.6 %reduce-scatter.2.cloned.1.call-start = ((), (), s32[]{:S(2)}) async-start(), calls=%async_computation.4 | async-start | bytes 7077888 | tf_op jit(solution)/shard_map/reduce_scatter | solution.py:41
  279.6 55.5 %copy-start.1 = (s32[4,8]{1,0:T(4,128)S(1)}, s32[4,8]{1,0:T(4,128)}, u32[]{:S(2)}) copy-start(s32[4,8]{1,0:T(4,128)} %param.13) | copy-start | bytes 388
  282.6 44.0 %all-to-all-start = ((s32[128,1,2]{2,1,0:T(1,128)}), s32[128,1,2]{2,1,0:T(1,128)S(1)}, u32[]{:S(2)}, u32[]{:S(2)}) async-start(s32[128,1,2]{2,1,0:T(1,128)} %bitcast.2), calls=%async_computation | async-start | bytes 131072 | tf_op jit(solution)/shard_map/all_to_all | solution.py:70
  326.6 34.4 %copy-start.3 = (f32[8,6]{1,0:T(8,128)S(1)}, f32[8,6]{1,0:T(8,128)}, u32[]{:S(2)}) copy-start(f32[8,6]{1,0:T(8,128)} %param.14) | copy-start | bytes 580
  326.6 34.7 %copy-start.2 = (f32[4,8]{1,0:T(4,128)S(1)}, f32[4,8]{1,0:T(4,128)}, u32[]{:S(2)}) copy-start(f32[4,8]{1,0:T(4,128)} %param.15) | copy-start | bytes 388
  326.6 32.6 %all-to-all-start.2 = ((bf16[128,2,3072]{2,1,0:T(2,128)(2,1)}), bf16[128,2,3072]{2,1,0:T(2,128)(2,1)S(1)}, u32[]{:S(2)}, u32[]{:S(2)}) async-start(bf16[128,2,3072]{2,1,0:T(2,128)(2,1)} %copy.25), calls=%async_computation.3 | async-start | bytes 3145728 | tf_op jit(solution)/shard_map/all_to_all | solution.py:63
Sparse Core Ops, SparseCore 0:
  279.7 41.3 reduce-scatter.1
